TPU v7x, 32 devices: a whole 2x2x4 slice. The times are simulated.
32 devices in a mesh: grp: 4 (over x, core), rel: 8 (over z, y).
Axes of the slice: x: 2, y: 2, z: 4, core: 2. Of those that a mesh axis runs over, the one named last changes fastest.
Arguments:
- head_ids: int32 [65536], P(('grp', 'rel')), may hold values from 0 to 1023
- relations: int32 [65536, 1], P(('grp', 'rel')), may hold values from 0 to 31; in each aligned block of 2048 rows (0 to 2047, 2048 to 4095, ...) at most 128 rows name the same one
- tail_ids: int32 [65536], P(('grp', 'rel')), may hold values from 0 to 1023
- neg_owner: int32 [1], replicated, may hold values from 0 to 31
- entities: bfloat16 [32768, 512], P(('grp', 'rel')), may hold values from -0.3984375 to 0.3984375
- rel_weight: float32 [32, 512, 512], P('rel'), may hold values from -6 to 6
- rel_accum: float32 [32, 512], P('rel'), may hold values from 0.001 to 0.1
Outputs:
- losses: bfloat16 [65536], P(('grp', 'rel'))
- head_grad: bfloat16 [65536, 512], P(('grp', 'rel'))
- new_rel: float32 [32, 512, 512], P('rel')
- new_accum: float32 [32, 512], P('rel')
Inputs may be any that keep to these rules, and one draw needn't show every extreme that they name: `head_ids`: a row of the device's own shard of 1024 entity rows. `tail_ids`: a row of the device's own shard of 1024 entity rows. `relations`: in the 2048 rows of one device no relation is named by more than 128 rows; some relation is named by exactly 128. `neg_owner`: a device index, counted grp first, then rel.
All inputs are finite; a program needn't handle non-finite values.
Results may differ from a plain program's by a relative error of at most 0.0095.
Values may be sent and summed in bfloat16 or wider, within the bound.
No kernel may reach another device: no remote copies, remote signals or barrier semaphores. Data moves between devices by JAX's collectives and lax.ppermute only.
A program may use at most 128 MiB of HBM per device.

v0:
```python
import jax
import jax.numpy as jnp
from jax import lax
from jax.sharding import PartitionSpec as P

LEARNING_RATE = 1.0


def broadcast(shard, axis, root):
    mine = lax.axis_index(axis) == root
    return lax.psum(jnp.where(mine, shard, jnp.zeros_like(shard)), axis)


def score_rows(query_rows, tail_rows, negatives):
    positive = jnp.sum(query_rows.astype(jnp.float32) * tail_rows.astype(jnp.float32), axis=-1)
    neg_scores = jnp.dot(query_rows, negatives.T, preferred_element_type=jnp.float32)
    losses = jax.nn.softplus(-positive) + jnp.mean(jax.nn.softplus(neg_scores), axis=-1)
    coefs = (jax.nn.sigmoid(neg_scores) / negatives.shape[0]).astype(jnp.bfloat16)
    grad_query = -jax.nn.sigmoid(-positive)[:, None] * tail_rows.astype(jnp.float32)
    grad_query = grad_query + jnp.dot(coefs, negatives, preferred_element_type=jnp.float32)
    return (losses.astype(jnp.bfloat16), grad_query.astype(jnp.bfloat16))


def adagrad(weight, accumulator, gradient):
    new_accum = accumulator + jnp.mean(gradient * gradient, axis=-1)
    return (weight - LEARNING_RATE * gradient / jnp.sqrt(new_accum)[..., None], new_accum)


def one_hot(ids, count):
    return (ids[:, None] == jnp.arange(count, dtype=jnp.int32)[None, :]).astype(jnp.bfloat16)


def select_rows(selector, rows):
    return jnp.dot(selector, rows, preferred_element_type=jnp.float32).astype(jnp.bfloat16)


def per_device(head_ids, relations, tail_ids, neg_owner, entities, rel_weight, rel_accum):
    rows_here = head_ids.shape[0]
    width = entities.shape[1]
    shard_rows = entities.shape[0]
    owner_count = lax.axis_size("rel")
    local_rels = rel_weight.shape[0]
    rel_count = owner_count * local_rels
    capacity = 2 * rows_here // rel_count
    layout = (owner_count, local_rels, capacity)
    slots = rel_count * capacity
    negatives = broadcast(entities, ("grp", "rel"), neg_owner[0])
    rel_ids = relations[:, 0]
    rel_hot = one_hot(rel_ids, rel_count)
    order = jnp.arange(rows_here, dtype=jnp.int32)
    lower = (order[:, None] >= order[None, :]).astype(jnp.bfloat16)
    running = jnp.dot(lower, rel_hot, preferred_element_type=jnp.float32)
    rank = jnp.sum(running * rel_hot.astype(jnp.float32), axis=-1).astype(jnp.int32) - 1
    position = rel_ids * capacity + rank
    ids = jnp.stack([head_ids, tail_ids], axis=-1) + 1
    slot_ids = jnp.zeros((slots, 2), jnp.int32).at[position].set(ids) - 1
    held_rows = select_rows(one_hot(slot_ids[:, 0], shard_rows), entities).reshape(
        layout + (width,)
    )
    held_rows = lax.all_to_all(held_rows, "rel", split_axis=0, concat_axis=0, tiled=True)
    tail_send = select_rows(one_hot(slot_ids[:, 1], shard_rows), entities).reshape(
        layout + (width,)
    )
    held_tails = lax.all_to_all(tail_send, "rel", split_axis=0, concat_axis=0, tiled=True)
    matrices = rel_weight.astype(jnp.bfloat16)
    projected = jnp.einsum(
        "srcd,rde->srce", held_rows, matrices, preferred_element_type=jnp.float32
    ).astype(jnp.bfloat16)
    slot_losses, slot_grads = score_rows(
        projected.reshape(-1, width), held_tails.reshape(-1, width), negatives
    )
    grad_rows = slot_grads.reshape(held_rows.shape)
    partial_value = jnp.einsum(
        "srcd,srce->rde", held_rows, grad_rows, preferred_element_type=jnp.float32
    )
    summed = lax.psum(partial_value.astype(jnp.bfloat16), "grp").astype(jnp.float32)
    head_back = jnp.einsum(
        "srce,rde->srcd", grad_rows, matrices, preferred_element_type=jnp.float32
    ).astype(jnp.bfloat16)
    per_owner = local_rels * capacity
    extra = -(-per_owner // width)
    loss_rows = slot_losses.reshape(owner_count, per_owner)
    loss_rows = jnp.pad(loss_rows, ((0, 0), (0, extra * width - per_owner)))
    loss_rows = loss_rows.reshape(owner_count, extra, width)
    packed = jnp.concatenate([head_back.reshape(owner_count, per_owner, width), loss_rows], axis=1)
    packed = lax.all_to_all(packed, "rel", split_axis=0, concat_axis=0, tiled=True)
    back_grads = packed[:, :per_owner].reshape(slots, width)
    back_losses = packed[:, per_owner:].reshape(owner_count, extra * width)
    back_losses = back_losses[:, :per_owner].reshape(slots)
    taken = one_hot(position, slots)
    head_grad = select_rows(taken, back_grads)
    losses = jnp.dot(taken, back_losses, preferred_element_type=jnp.float32).astype(jnp.bfloat16)
    new_rel, new_accum = adagrad(rel_weight, rel_accum, summed)
    return (losses, head_grad, new_rel, new_accum)


def solution(mesh):
    placed = (
        P(("grp", "rel")),
        P(("grp", "rel"), None),
        P(("grp", "rel")),
        P(),
        P(("grp", "rel"), None),
        P("rel", None, None),
        P("rel", None),
    )
    return jax.shard_map(
        per_device,
        mesh=mesh,
        in_specs=placed,
        out_specs=(
            P(("grp", "rel")),
            P(("grp", "rel"), None),
            P("rel", None, None),
            P("rel", None),
        ),
        check_vma=False,
    )
```

profile of v0, /device:TPU:0, one launch (start us, length us, event | category | flops | bytes accessed | tf_op | source)
XLA Modules:
  0.0 491.5 jit_solution(8501658927828690532)
XLA Ops:
  7.2 0.0 copy-start.3
  7.2 0.0 copy-start.4
  7.2 0.0 copy-start.5
  7.2 2.3 fusion.29
  9.5 0.0 copy-done.3
  9.5 0.0 copy-done.4
  9.5 0.0 copy-done.5
  9.6 0.4 copy.56
  9.9 6.1 %scatter_custom_fusion = s32[4096,2]{1,0:T(8,128)S(1)} fusion(s32[2048]{0:T(1024)S(1)} %bitcast.78, s32[2048,2]{1,0:T(8,128)S(1)} %copy.56, s32[]{:T(128)} %constant.17.clone.1), kind=kCustom, calls=%fused_computation.47 | custom fusion | bytes 32772 | tf_op jit(solution)/shard_map/scatter | solution.py:56
  16.0 0.0 copy-start.2
  16.1 0.1 broadcast_add_fusion
  16.2 1.7 slice_reduce_fusion
  17.9 0.0 copy-done.2
  17.9 6.2 %fusion.13 = bf16[4096,512]{1,0:T(8,128)(2,1)} fusion(bf16[1024,512]{1,0:T(8,128)(2,1)S(1)} %copy-done.2, s32[4096]{0:T(1024)S(1)} %get-tuple-element.4), kind=kOutput, calls=%fused_computation.22 | convolution fusion | flops 4301258752 | bytes 5259264 | tf_op jit(solution)/shard_map/dot_general | solution.py:34
  24.2 7.3 %all-to-all-start.1 = ((bf16[8,4,128,512]{3,2,1,0:T(8,128)(2,1)}), bf16[8,4,128,512]{3,2,1,0:T(8,128)(2,1)}, u32[]{:S(2)}, u32[]{:S(2)}) async-start(bf16[8,4,128,512]{3,2,1,0:T(8,128)(2,1)} %bitcast.67), calls=%async_computation.1 | async-start | bytes 8388608 | tf_op jit(solution)/shard_map/all_to_all | solution.py:64
  31.5 6.2 %fusion.14 = bf16[4096,512]{1,0:T(8,128)(2,1)} fusion(bf16[1024,512]{1,0:T(8,128)(2,1)S(1)} %copy-done.2, s32[4096]{0:T(1024)S(1)} %get-tuple-element.5), kind=kOutput, calls=%fused_computation.23 | convolution fusion | flops 4301258752 | bytes 5259264 | tf_op jit(solution)/shard_map/dot_general | solution.py:34
  37.7 87.0 %all-to-all-done.1 = bf16[8,4,128,512]{3,2,1,0:T(8,128)(2,1)} async-done(((bf16[8,4,128,512]{3,2,1,0:T(8,128)(2,1)}), bf16[8,4,128,512]{3,2,1,0:T(8,128)(2,1)}, u32[]{:S(2)}, u32[]{:S(2)}) %all-to-all-start.1) | async-done | bytes 4194336 | tf_op jit(solution)/shard_map/all_to_all | solution.py:64
  124.8 4.6 all-to-all-start
  129.4 10.9 %all-reduce.3.cloned.1.call-start = ((), (), s32[]{:S(2)}) async-start(), calls=%async_computation.3 | async-start | bytes 2097152 | tf_op jit(solution)/shard_map/psum | solution.py:11
  140.9 1.0 broadcast_select_fusion
  142.0 0.0 all-reduce.3.cloned.1.call-update
  142.0 84.8 %all-to-all-done = bf16[8,4,128,512]{3,2,1,0:T(8,128)(2,1)} async-done(((bf16[8,4,128,512]{3,2,1,0:T(8,128)(2,1)}), bf16[8,4,128,512]{3,2,1,0:T(8,128)(2,1)}, u32[]{:S(2)}, u32[]{:S(2)}) %all-to-all-start) | async-done | bytes 4194336 | tf_op jit(solution)/shard_map/all_to_all | solution.py:60
  226.8 7.2 %multiply_reduce_fusion = (f32[8,4,128]{2,0,1:T(8,128)S(1)}, bf16[8,4,128,512]{3,2,0,1:T(8,128)(2,1)S(1)}) fusion(bf16[8,4,128,512]{3,2,1,0:T(8,128)(2,1)} %all-to-all-done.1, f32[4,512,512]{2,1,0:T(8,128)} %param.12, bf16[8,4,128,512]{3,2,1,0:T(8,128)(2,1)} %all-to-all-done), kind=kOutput, calls=%fused_computation.18 | convolution fusion | flops 2159013888 | bytes 16793600 | tf_op jit(solution)/shard_map/srcd,rde->srce/dot_general | solution.py:66
  234.0 2.5 copy.61
  236.5 3.4 copy_convert_fusion
  239.9 4.2 copy.60
  244.1 82.8 %all-reduce.3.cloned.1.call-done = bf16[1024,512]{1,0:T(8,128)(2,1)} async-done(((bf16[1024,512]{1,0:T(8,128)(2,1)}), bf16[1024,512]{1,0:T(8,128)(2,1)}) %all-reduce.3.cloned.1.call-update) | async-done | bytes 1048592 | tf_op jit(solution)/shard_map/psum | solution.py:11
  326.9 16.2 %fusion.2 = (f32[4096]{0:T(1024)S(1)}, f32[4096,1024]{0,1:T(8,128)}) fusion(bf16[4096,512]{1,0:T(8,128)(2,1)} %bitcast.66, bf16[1024,512]{1,0:T(8,128)(2,1)} %all-reduce.3.cloned.1.call-done), kind=kOutput, calls=%fused_computation.5 | convolution fusion | flops 4324323328 | bytes 22036480 | tf_op jit(solution)/shard_map/dot_general | solution.py:16
  343.1 0.0 copy-done
  343.1 10.8 %fusion.9 = bf16[4096,512]{1,0:T(8,128)(2,1)} fusion(f32[8,4,128,512]{3,2,1,0:T(8,128)S(1)} %copy-done, bf16[1024,512]{1,0:T(8,128)(2,1)S(1)} %copy-done.7, f32[4096,1024]{0,1:T(8,128)} %get-tuple-element.11, f32[4096]{0:T(1024)S(1)} %bitcast.70), kind=kOutput, calls=%fused_computation.17 | convolution fusion | flops 4322230272 | bytes 30425088 | tf_op jit(solution)/shard_map/dot_general | solution.py:20
  354.0 4.6 convert_bitcast_fusion
  358.6 2.2 copy.63
  360.9 4.6 pad_maximum_fusion
  365.5 4.6 all-to-all-start.2
  370.1 0.2 all-reduce.5.cloned.1.call-start
  370.3 7.2 %bitcast_convert_fusion = bf16[4,512,512]{2,1,0:T(8,128)(2,1)} fusion(bf16[8,4,128,512]{3,2,1,0:T(8,128)(2,1)} %all-to-all-done, bf16[8,4,128,512]{3,2,1,0:T(8,128)(2,1)} %bitcast.80), kind=kOutput, calls=%fused_computation.29 | convolution fusion | flops 2148532224 | bytes 10485760 | tf_op jit(solution)/shard_map/srcd,srce->rde/dot_general | solution.py:73
  377.4 0.0 all-reduce.5.cloned.1.call-update
  377.5 52.6 %all-reduce.5.cloned.1.call-done = bf16[4,512,512]{2,1,0:T(8,128)(2,1)} async-done(((bf16[4,512,512]{2,1,0:T(8,128)(2,1)}), bf16[4,512,512]{2,1,0:T(8,128)(2,1)}) %all-reduce.5.cloned.1.call-update) | async-done | bytes 2097168 | tf_op jit(solution)/shard_map/psum | solution.py:76
  430.1 2.1 fusion.15
  432.2 0.0 copy-done.6
  432.2 0.6 fusion.44
  432.8 5.5 %fusion.16 = f32[4,512,512]{2,1,0:T(8,128)} fusion(f32[4,512,512]{2,1,0:T(8,128)} %param.12, bf16[4,512,512]{2,1,0:T(8,128)(2,1)} %all-reduce.5.cloned.1.call-done, f32[4,512]{1,0:T(4,128)S(1)} %get-tuple-element.6), kind=kLoop, calls=%fused_computation.28 | loop fusion | flops 3145728 | bytes 10493952 | tf_op jit(solution)/shard_map/sub | solution.py:26
  438.3 25.8 %all-to-all-done.2 = bf16[8,513,512]{2,1,0:T(8,128)(2,1)} async-done(((bf16[8,513,512]{2,1,0:T(8,128)(2,1)}), bf16[8,513,512]{2,1,0:T(8,128)(2,1)}, u32[]{:S(2)}, u32[]{:S(2)}) %all-to-all-start.2) | async-done | bytes 4202528 | tf_op jit(solution)/shard_map/all_to_all | solution.py:86
  464.0 2.5 slice.19
  466.5 10.1 %fusion.21 = bf16[2048,512]{1,0:T(8,128)(2,1)} fusion(bf16[4096,512]{1,0:T(8,128)(2,1)S(1)} %bitcast.68, s32[2048]{0:T(1024)S(1)} %bitcast.76), kind=kOutput, calls=%fused_computation.37 | convolution fusion | flops 8599371776 | bytes 6299648 | tf_op jit(solution)/shard_map/dot_general | solution.py:34
  476.6 0.8 slice.18
  477.4 6.2 %fusion.1 = f32[1,2048]{1,0:T(1,128)S(1)} fusion(bf16[4096,1]{0,1:T(2,128)(2,1)S(1)} %bitcast.71, s32[2048]{0:T(1024)S(1)} %bitcast.77), kind=kOutput, calls=%fused_computation.4 | convolution fusion | flops 25165824 | bytes 24576 | tf_op jit(solution)/shard_map/dot_general | solution.py:92
  483.7 0.6 convert_element_type.102
  (15 shorter events, 0.1 us)
Async XLA Ops:
  7.2 2.3 copy-start.3
  7.2 2.3 copy-start.4
  7.2 2.3 copy-start.5
  16.0 1.9 copy-start.2
  24.2 100.6 %all-to-all-start.1 = ((bf16[8,4,128,512]{3,2,1,0:T(8,128)(2,1)}), bf16[8,4,128,512]{3,2,1,0:T(8,128)(2,1)}, u32[]{:S(2)}, u32[]{:S(2)}) async-start(bf16[8,4,128,512]{3,2,1,0:T(8,128)(2,1)} %bitcast.67), calls=%async_computation.1 | async-start | bytes 8388608 | tf_op jit(solution)/shard_map/all_to_all | solution.py:64
  124.8 102.0 %all-to-all-start = ((bf16[8,4,128,512]{3,2,1,0:T(8,128)(2,1)}), bf16[8,4,128,512]{3,2,1,0:T(8,128)(2,1)}, u32[]{:S(2)}, u32[]{:S(2)}) async-start(bf16[8,4,128,512]{3,2,1,0:T(8,128)(2,1)} %bitcast.65), calls=%async_computation | async-start | bytes 8388608 | tf_op jit(solution)/shard_map/all_to_all | solution.py:60
  129.4 197.5 %all-reduce.3.cloned.1.call-start = ((), (), s32[]{:S(2)}) async-start(), calls=%async_computation.3 | async-start | bytes 2097152 | tf_op jit(solution)/shard_map/psum | solution.py:11
  326.9 16.2 %copy-start = (f32[8,4,128,512]{3,2,1,0:T(8,128)S(1)}, f32[8,4,128,512]{3,2,1,0:T(8,128)}, u32[]{:S(2)}) copy-start(f32[8,4,128,512]{3,2,1,0:T(8,128)} %copy.60) | copy-start | bytes 25165828
  326.9 16.2 %copy-start.7 = (bf16[1024,512]{1,0:T(8,128)(2,1)S(1)}, bf16[1024,512]{1,0:T(8,128)(2,1)}, u32[]{:S(2)}) copy-start(bf16[1024,512]{1,0:T(8,128)(2,1)} %all-reduce.3.cloned.1.call-done) | copy-start | bytes 3145732
  343.1 10.8 %copy-start.1 = (f32[4,512,512]{2,1,0:T(8,128)S(1)}, f32[4,512,512]{2,1,0:T(8,128)}, u32[]{:S(2)}) copy-start(f32[4,512,512]{2,1,0:T(8,128)} %param.12) | copy-start | bytes 12582916
  365.5 98.6 %all-to-all-start.2 = ((bf16[8,513,512]{2,1,0:T(8,128)(2,1)}), bf16[8,513,512]{2,1,0:T(8,128)(2,1)}, u32[]{:S(2)}, u32[]{:S(2)}) async-start(bf16[8,513,512]{2,1,0:T(8,128)(2,1)} %pad_maximum_fusion), calls=%async_computation.2 | async-start | bytes 8519680 | tf_op jit(solution)/shard_map/all_to_all | solution.py:86
  370.1 60.0 %all-reduce.5.cloned.1.call-start = ((), (), s32[]{:S(2)}) async-start(), calls=%async_computation.4 | async-start | bytes 4194304 | tf_op jit(solution)/shard_map/psum | solution.py:76
  377.4 54.7 %copy-start.6 = (f32[4,512]{1,0:T(4,128)S(1)}, f32[4,512]{1,0:T(4,128)}, u32[]{:S(2)}) copy-start(f32[4,512]{1,0:T(4,128)} %param.13) | copy-start | bytes 24580
Sparse Core Ops, SparseCore 0:
  142.1 184.7 all-reduce.2
  377.6 52.4 all-reduce.4
where the time goes:
time: 499 us; the launch traced here: 491 us
  waiting for transfers between devices  333 us (67%)
  matrix products  77 us (15%)
  starting transfers between devices  27.6 us (6%)
  local copies, waits for them, and re-layouts  20.5 us (4%)
  other arithmetic  18 us (4%)
  between operations  15.3 us (3%)
    all_to_all x1, waiting for transfers between devices, per_device(): lax.all_to_all(tail_send, 'rel', split_axis=0, concat_axis=0, tiled=True)  87 us
    all_to_all x1, waiting for transfers between devices, per_device(): lax.all_to_all(held_rows, 'rel', split_axis=0, concat_axis=0, tiled=True)  84.8 us
    psum x1, waiting for transfers between devices, broadcast(): return lax.psum(jnp.where(mine, shard, jnp.zeros_like(shard)), axis)  82.8 us
    psum x1, waiting for transfers between devices, per_device(): lax.psum(partial_value.astype(jnp.bfloat16), 'grp').astype(jnp.float32)  52.6 us
    all_to_all x1, waiting for transfers between devices, per_device(): lax.all_to_all(packed, 'rel', split_axis=0, concat_axis=0, tiled=True)  25.8 us
    dot_general x3, matrix products, select_rows(): jnp.dot(selector, rows, preferred_element_type=jnp.float32)  22.5 us
    dot_general x1, matrix products, score_rows(): jnp.dot(query_rows, negatives.T, preferred_element_type=jnp.float32)  16.2 us
    psum x1, starting transfers between devices, broadcast(): return lax.psum(jnp.where(mine, shard, jnp.zeros_like(shard)), axis)  10.9 us
  transfers between devices with their start and end apart: 5, of which 5 were waited for; matrix products, arithmetic and copies ran while one was open for 8% of the time, Pallas kernels for 0%

commit v1 on v0

--- a/solution.py
+++ b/solution.py
@@ -61,7 +61,24 @@
     tail_send = select_rows(one_hot(slot_ids[:, 1], shard_rows), entities).reshape(
         layout + (width,)
     )
-    held_tails = lax.all_to_all(tail_send, "rel", split_axis=0, concat_axis=0, tiled=True)
+    carry_in, r1 = (lax.psum(1, "rel"), lax.axis_index("rel"))
+    long_array = tail_send.shape[0] // carry_in
+    p_next = list(tail_send.shape)
+    p_next[0] = long_array
+    v_now = p_next[0]
+    p_next[0] = v_now * carry_in
+    jj = 0
+    held_tails = jnp.zeros(p_next, tail_send.dtype)
+    while jj < carry_in:
+        found_now = lax.dynamic_slice_in_dim(tail_send, (r1 ^ jj) * long_array, long_array, axis=0)
+        if jj:
+            found_now = lax.ppermute(
+                found_now, axis_name="rel", perm=tuple(((t, t ^ jj) for t in range(carry_in)))
+            )
+        held_tails = lax.dynamic_update_slice_in_dim(
+            held_tails, found_now, (r1 ^ jj) * v_now, axis=0
+        )
+        jj = jj + 1
     matrices = rel_weight.astype(jnp.bfloat16)
     projected = jnp.einsum(
         "srcd,rde->srce", held_rows, matrices, preferred_element_type=jnp.float32

time: 499 us -> 448 us (0.90)
  waiting for transfers between devices: 333 us -> 282 us
  local copies, waits for them, and re-layouts: 20.5 us -> 31.1 us
  other arithmetic: 18 us -> 12.3 us
    ppermute x0 -> x7, waiting for transfers between devices: none -> 138 us  [per_device(): lax.ppermute(found_now, axis_name='rel', perm=tuple(((t, t ^ jj) for t in...]
    all_to_all x1 -> x0, waiting for transfers between devices: 87 us -> none  [per_device(): lax.all_to_all(tail_send, 'rel', split_axis=0, concat_axis=0, tiled=True)]
    all_to_all x1, waiting for transfers between devices: 84.8 us -> 0.01 us  [per_device(): lax.all_to_all(held_rows, 'rel', split_axis=0, concat_axis=0, tiled=True)]
    psum x1, waiting for transfers between devices: 82.8 us -> 65.6 us  [broadcast(): return lax.psum(jnp.where(mine, shard, jnp.zeros_like(shard)), axis)]
    ppermute x0 -> x7, starting transfers between devices: none -> 13.3 us  [per_device(): lax.ppermute(found_now, axis_name='rel', perm=tuple(((t, t ^ jj) for t in...]
    psum x1, starting transfers between devices: 10.9 us -> 0.5 us  [broadcast(): return lax.psum(jnp.where(mine, shard, jnp.zeros_like(shard)), axis)]
    all_to_all x1 -> x0, starting transfers between devices: 7.31 us -> none  [per_device(): lax.all_to_all(tail_send, 'rel', split_axis=0, concat_axis=0, tiled=True)]
    dynamic_update_slice x0 -> x8, local copies, waits for them, and re-layouts: none -> 6.55 us  [per_device(): lax.dynamic_update_slice_in_dim(held_tails, found_now, (r1 ^ jj) * v_now,...]
  transfers between devices with their start and end apart: 5 -> 11, of which waited for: 5 -> 8; matrix products, arithmetic and copies ran while one was open for 8% -> 10% of each run, Pallas kernels for 0% -> 0%
where the time goes in v1:
time: 448 us; the launch traced here: 442 us
  waiting for transfers between devices  282 us (63%)
  matrix products  75.2 us (17%)
  local copies, waits for them, and re-layouts  31.1 us (7%)
  starting transfers between devices  25.7 us (6%)
  between operations  15.3 us (3%)
  other arithmetic  12.3 us (3%)
    ppermute x7, waiting for transfers between devices, per_device(): lax.ppermute(found_now, axis_name='rel', perm=tuple(((t, t ^ jj) for t in...  138 us
    psum x1, waiting for transfers between devices, broadcast(): return lax.psum(jnp.where(mine, shard, jnp.zeros_like(shard)), axis)  65.6 us
    psum x1, waiting for transfers between devices, per_device(): lax.psum(partial_value.astype(jnp.bfloat16), 'grp').astype(jnp.float32)  52.8 us
    all_to_all x1, waiting for transfers between devices, per_device(): lax.all_to_all(packed, 'rel', split_axis=0, concat_axis=0, tiled=True)  25.8 us
    dot_general x3, matrix products, select_rows(): jnp.dot(selector, rows, preferred_element_type=jnp.float32)  21.9 us
    dot_general x1, matrix products, score_rows(): jnp.dot(query_rows, negatives.T, preferred_element_type=jnp.float32)  16.5 us
    ppermute x7, starting transfers between devices, per_device(): lax.ppermute(found_now, axis_name='rel', perm=tuple(((t, t ^ jj) for t in...  13.3 us
    dot_general x1, matrix products, score_rows(): jnp.dot(coefs, negatives, preferred_element_type=jnp.float32)  11.5 us
  transfers between devices with their start and end apart: 11, of which 8 were waited for; matrix products, arithmetic and copies ran while one was open for 10% of the time, Pallas kernels for 0%

profile of v1, /device:TPU:0, one launch (start us, length us, event | category | flops | bytes accessed | tf_op | source)
XLA Modules:
  0.0 442.1 jit_solution(15120559767810166360)
XLA Ops:
  7.2 2.3 fusion.29
  9.9 6.1 %scatter_custom_fusion = s32[4096,2]{1,0:T(8,128)S(1)} fusion(s32[2048]{0:T(1024)S(1)} %bitcast.94, s32[2048,2]{1,0:T(8,128)S(1)} %copy.84, s32[]{:T(128)} %constant.23.clone.1), kind=kCustom, calls=%fused_computation.46 | custom fusion | bytes 32772 | tf_op jit(solution)/shard_map/scatter | solution.py:56
  16.2 1.7 slice_reduce_fusion
  17.9 6.2 %fusion.14 = bf16[4096,512]{1,0:T(8,128)(2,1)} fusion(bf16[1024,512]{1,0:T(8,128)(2,1)S(1)} %copy-done.3, s32[4096]{0:T(1024)S(1)} %get-tuple-element.5), kind=kOutput, calls=%fused_computation.23 | convolution fusion | flops 4301258752 | bytes 5259264 | tf_op jit(solution)/shard_map/dot_general | solution.py:34
  24.1 7.3 %all-to-all-start = ((bf16[8,4,128,512]{3,2,1,0:T(8,128)(2,1)}), bf16[8,4,128,512]{3,2,1,0:T(8,128)(2,1)}, u32[]{:S(2)}, u32[]{:S(2)}) async-start(bf16[8,4,128,512]{3,2,1,0:T(8,128)(2,1)} %bitcast.82), calls=%async_computation | async-start | bytes 8388608 | tf_op jit(solution)/shard_map/all_to_all | solution.py:60
  31.5 0.5 all-reduce.3.cloned.1.call-start
  32.0 5.6 %fusion.13 = bf16[4096,512]{1,0:T(8,128)(2,1)S(1)} fusion(bf16[1024,512]{1,0:T(8,128)(2,1)S(1)} %copy-done.3, s32[4096]{0:T(1024)S(1)} %get-tuple-element.4), kind=kOutput, calls=%fused_computation.22 | convolution fusion | flops 4301258752 | bytes 5259264 | tf_op jit(solution)/shard_map/dot_general | solution.py:34
  37.6 2.0 copy-done.1
  39.6 1.2 dynamic-slice_bitcast_fusion
  40.8 2.0 collective-permute-start
  42.8 1.5 collective-permute-start.1
  44.3 2.9 collective-permute-start.3
  47.2 1.5 collective-permute-start.4
  49.3 1.0 broadcast_select_fusion
  50.9 1.1 bitcast_dynamic-update-slice_fusion
  52.0 28.1 %collective-permute-done = bf16[1,4,128,512]{3,2,0,1:T(8,128)(2,1)} collective-permute-done((bf16[1,4,128,512]{3,2,0,1:T(8,128)(2,1)}, bf16[1,4,128,512]{3,2,0,1:T(8,128)(2,1)}, u32[]{:S(2)}, u32[]{:S(2)}) %collective-permute-start) | collective-permute-done | bytes 524320 | tf_op jit(solution)/shard_map/ppermute | solution.py:75
  80.1 1.8 collective-permute-start.5
  81.8 1.1 constant_dynamic-update-slice_fusion.6
  82.9 34.5 %collective-permute-done.1 = bf16[1,4,128,512]{3,2,0,1:T(8,128)(2,1)} collective-permute-done((bf16[1,4,128,512]{3,2,0,1:T(8,128)(2,1)}, bf16[1,4,128,512]{3,2,0,1:T(8,128)(2,1)}, u32[]{:S(2)}, u32[]{:S(2)}) %collective-permute-start.1) | collective-permute-done | bytes 524320 | tf_op jit(solution)/shard_map/ppermute | solution.py:75
  117.5 3.7 collective-permute-start.6
  121.1 1.1 constant_dynamic-update-slice_fusion.5
  122.2 6.5 %collective-permute-done.2 = bf16[1,4,128,512]{3,2,0,1:T(8,128)(2,1)} collective-permute-done((bf16[1,4,128,512]{3,2,0,1:T(8,128)(2,1)}, bf16[1,4,128,512]{3,2,0,1:T(8,128)(2,1)}, u32[]{:S(2)}, u32[]{:S(2)}) %collective-permute-start.2) | collective-permute-done | bytes 524320 | tf_op jit(solution)/shard_map/ppermute | solution.py:75
  128.7 1.1 constant_dynamic-update-slice_fusion.4
  129.8 58.5 %collective-permute-done.3 = bf16[1,4,128,512]{3,2,0,1:T(8,128)(2,1)} collective-permute-done((bf16[1,4,128,512]{3,2,0,1:T(8,128)(2,1)S(1)}, bf16[1,4,128,512]{3,2,0,1:T(8,128)(2,1)}, u32[]{:S(2)}, u32[]{:S(2)}) %collective-permute-start.3) | collective-permute-done | bytes 524320 | tf_op jit(solution)/shard_map/ppermute | solution.py:75
  188.3 1.1 constant_dynamic-update-slice_fusion.3
  189.3 10.7 %collective-permute-done.4 = bf16[1,4,128,512]{3,2,0,1:T(8,128)(2,1)} collective-permute-done((bf16[1,4,128,512]{3,2,0,1:T(8,128)(2,1)S(1)}, bf16[1,4,128,512]{3,2,0,1:T(8,128)(2,1)}, u32[]{:S(2)}, u32[]{:S(2)}) %collective-permute-start.4) | collective-permute-done | bytes 524320 | tf_op jit(solution)/shard_map/ppermute | solution.py:75
  200.0 1.1 constant_dynamic-update-slice_fusion.2
  201.2 2.0 copy-done
  203.3 4.4 copy.95
  207.6 7.1 %multiply_reduce_fusion = (f32[8,4,128]{2,0,1:T(8,128)S(1)}, bf16[8,4,128,512]{3,2,0,1:T(8,128)(2,1)S(1)}) fusion(bf16[8,4,128,512]{3,2,0,1:T(8,128)(2,1)} %copy-done, f32[4,512,512]{2,1,0:T(8,128)} %param.12, bf16[8,4,128,512]{3,2,1,0:T(8,128)(2,1)} %all-to-all-done), kind=kOutput, calls=%fused_computation.18 | convolution fusion | flops 2159013888 | bytes 16793600 | tf_op jit(solution)/shard_map/srcd,rde->srce/dot_general | solution.py:83
  214.8 2.5 copy.96
  217.2 65.6 %all-reduce.3.cloned.1.call-done = bf16[1024,512]{1,0:T(8,128)(2,1)} async-done(((bf16[1024,512]{1,0:T(8,128)(2,1)}), bf16[1024,512]{1,0:T(8,128)(2,1)}) %all-reduce.3.cloned.1.call-update) | async-done | bytes 1048592 | tf_op jit(solution)/shard_map/psum | solution.py:11
  282.8 16.5 %fusion.2 = (f32[4096]{0:T(1024)S(1)}, f32[4096,1024]{0,1:T(8,128)}) fusion(bf16[4096,512]{1,0:T(8,128)(2,1)} %bitcast.83, bf16[1024,512]{1,0:T(8,128)(2,1)} %all-reduce.3.cloned.1.call-done), kind=kOutput, calls=%fused_computation.5 | convolution fusion | flops 4324323328 | bytes 22036480 | tf_op jit(solution)/shard_map/dot_general | solution.py:16
  299.4 11.5 %fusion.9 = bf16[4096,512]{1,0:T(8,128)(2,1)S(1)} fusion(f32[8,4,128,512]{3,2,1,0:T(8,128)} %copy.95, bf16[1024,512]{1,0:T(8,128)(2,1)S(1)} %copy-done.8, f32[4096,1024]{0,1:T(8,128)} %get-tuple-element.18, f32[4096]{0:T(1024)S(1)} %bitcast.86), kind=kOutput, calls=%fused_computation.17 | convolution fusion | flops 4322230272 | bytes 30425088 | tf_op jit(solution)/shard_map/dot_general | solution.py:20
  311.0 2.4 convert_bitcast_fusion
  313.8 2.3 pad_maximum_fusion
  316.1 4.5 %all-to-all-start.1 = ((bf16[8,513,512]{2,1,0:T(8,128)(2,1)}), bf16[8,513,512]{2,1,0:T(8,128)(2,1)}, u32[]{:S(2)}, u32[]{:S(2)}) async-start(bf16[8,513,512]{2,1,0:T(8,128)(2,1)} %pad_maximum_fusion), calls=%async_computation.1 | async-start | bytes 8519680 | tf_op jit(solution)/shard_map/all_to_all | solution.py:103
  320.7 7.2 %bitcast_convert_fusion = bf16[4,512,512]{2,1,0:T(8,128)(2,1)} fusion(bf16[8,4,128,512]{3,2,1,0:T(8,128)(2,1)} %all-to-all-done, bf16[8,4,128,512]{3,2,1,0:T(8,128)(2,1)} %bitcast.96), kind=kOutput, calls=%fused_computation.29 | convolution fusion | flops 2148532224 | bytes 10485760 | tf_op jit(solution)/shard_map/srcd,srce->rde/dot_general | solution.py:90
  327.9 52.8 %all-reduce.5.cloned.1.call-done = bf16[4,512,512]{2,1,0:T(8,128)(2,1)} async-done(((bf16[4,512,512]{2,1,0:T(8,128)(2,1)}), bf16[4,512,512]{2,1,0:T(8,128)(2,1)}) %all-reduce.5.cloned.1.call-update) | async-done | bytes 2097168 | tf_op jit(solution)/shard_map/psum | solution.py:93
  380.7 2.1 fusion.15
  382.7 0.6 fusion.44
  383.4 5.5 %fusion.16 = f32[4,512,512]{2,1,0:T(8,128)} fusion(f32[4,512,512]{2,1,0:T(8,128)} %param.12, bf16[4,512,512]{2,1,0:T(8,128)(2,1)} %all-reduce.5.cloned.1.call-done, f32[4,512]{1,0:T(4,128)S(1)} %get-tuple-element.6), kind=kLoop, calls=%fused_computation.28 | loop fusion | flops 3145728 | bytes 10493952 | tf_op jit(solution)/shard_map/sub | solution.py:26
  388.9 25.8 %all-to-all-done.1 = bf16[8,513,512]{2,1,0:T(8,128)(2,1)} async-done(((bf16[8,513,512]{2,1,0:T(8,128)(2,1)}), bf16[8,513,512]{2,1,0:T(8,128)(2,1)}, u32[]{:S(2)}, u32[]{:S(2)}) %all-to-all-start.1) | async-done | bytes 4202528 | tf_op jit(solution)/shard_map/all_to_all | solution.py:103
  414.6 0.9 slice.18
  415.5 6.4 %fusion.1 = f32[1,2048]{1,0:T(1,128)S(1)} fusion(bf16[4096,1]{0,1:T(2,128)(2,1)S(1)} %bitcast.87, s32[2048]{0:T(1024)S(1)} %bitcast.92), kind=kOutput, calls=%fused_computation.4 | convolution fusion | flops 25165824 | bytes 24576 | tf_op jit(solution)/shard_map/dot_general | solution.py:109
  421.9 0.6 convert_element_type.102
  422.5 2.5 slice.19
  425.0 10.1 %fusion.21 = bf16[2048,512]{1,0:T(8,128)(2,1)} fusion(bf16[4096,512]{1,0:T(8,128)(2,1)S(1)} %bitcast.84, s32[2048]{0:T(1024)S(1)} %bitcast.93), kind=kOutput, calls=%fused_computation.36 | convolution fusion | flops 8599371776 | bytes 6299648 | tf_op jit(solution)/shard_map/dot_general | solution.py:34
  (40 shorter events, 1.8 us)
Async XLA Ops:
  7.2 2.3 copy-start.4
  7.2 2.3 copy-start.5
  7.2 2.3 copy-start.6
  16.0 1.9 copy-start.3
  24.1 183.5 %all-to-all-start = ((bf16[8,4,128,512]{3,2,1,0:T(8,128)(2,1)}), bf16[8,4,128,512]{3,2,1,0:T(8,128)(2,1)}, u32[]{:S(2)}, u32[]{:S(2)}) async-start(bf16[8,4,128,512]{3,2,1,0:T(8,128)(2,1)} %bitcast.82), calls=%async_computation | async-start | bytes 8388608 | tf_op jit(solution)/shard_map/all_to_all | solution.py:60
  31.5 251.4 %all-reduce.3.cloned.1.call-start = ((), (), s32[]{:S(2)}) async-start(), calls=%async_computation.2 | async-start | bytes 2097152 | tf_op jit(solution)/shard_map/psum | solution.py:11
  37.6 2.0 copy-start.1
  40.8 39.2 %collective-permute-start = (bf16[1,4,128,512]{3,2,0,1:T(8,128)(2,1)}, bf16[1,4,128,512]{3,2,0,1:T(8,128)(2,1)}, u32[]{:S(2)}, u32[]{:S(2)}) collective-permute-start(bf16[1,4,128,512]{3,2,0,1:T(8,128)(2,1)} %get-tuple-element.16), channel_id=1, source_target_pairs={{0,1},{1,0},{2,3},{3,2},{4,5},{5,4},{6,7},{7,6},{8,9},{9,8},{10,11... | collective-permute-start | bytes 1572872 | tf_op jit(solution)/shard_map/ppermute | solution.py:75
  42.8 74.6 %collective-permute-start.1 = (bf16[1,4,128,512]{3,2,0,1:T(8,128)(2,1)}, bf16[1,4,128,512]{3,2,0,1:T(8,128)(2,1)}, u32[]{:S(2)}, u32[]{:S(2)}) collective-permute-start(bf16[1,4,128,512]{3,2,0,1:T(8,128)(2,1)} %get-tuple-element.15), channel_id=1, source_target_pairs={{0,2},{1,3},{2,0},{3,1},{4,6},{5,7},{6,4},{7,5},{8,10},{9,11},{10,... | collective-permute-start | bytes 1572872 | tf_op jit(solution)/shard_map/ppermute | solution.py:75
  44.3 84.4 %collective-permute-start.2 = (bf16[1,4,128,512]{3,2,0,1:T(8,128)(2,1)}, bf16[1,4,128,512]{3,2,0,1:T(8,128)(2,1)}, u32[]{:S(2)}, u32[]{:S(2)}) collective-permute-start(bf16[1,4,128,512]{3,2,0,1:T(8,128)(2,1)} %get-tuple-element.14), channel_id=1, source_target_pairs={{0,3},{1,2},{2,1},{3,0},{4,7},{5,6},{6,5},{7,4},{8,11},{9,10},{10,... | collective-permute-start | bytes 1572872 | tf_op jit(solution)/shard_map/ppermute | solution.py:75
  44.3 143.9 %collective-permute-start.3 = (bf16[1,4,128,512]{3,2,0,1:T(8,128)(2,1)S(1)}, bf16[1,4,128,512]{3,2,0,1:T(8,128)(2,1)}, u32[]{:S(2)}, u32[]{:S(2)}) collective-permute-start(bf16[1,4,128,512]{3,2,0,1:T(8,128)(2,1)S(1)} %get-tuple-element.13), channel_id=1, source_target_pairs={{0,4},{1,5},{2,6},{3,7},{4,0},{5,1},{6,2},{7,3},{8,12},{9,13},{10,... | collective-permute-start | bytes 1572872 | tf_op jit(solution)/shard_map/ppermute | solution.py:75
  47.2 152.8 %collective-permute-start.4 = (bf16[1,4,128,512]{3,2,0,1:T(8,128)(2,1)S(1)}, bf16[1,4,128,512]{3,2,0,1:T(8,128)(2,1)}, u32[]{:S(2)}, u32[]{:S(2)}) collective-permute-start(bf16[1,4,128,512]{3,2,0,1:T(8,128)(2,1)S(1)} %get-tuple-element.12), channel_id=1, source_target_pairs={{0,5},{1,4},{2,7},{3,6},{4,1},{5,0},{6,3},{7,2},{8,13},{9,12},{10,... | collective-permute-start | bytes 1572872 | tf_op jit(solution)/shard_map/ppermute | solution.py:75
  80.1 121.0 %collective-permute-start.5 = (bf16[1,4,128,512]{3,2,0,1:T(8,128)(2,1)S(1)}, bf16[1,4,128,512]{3,2,0,1:T(8,128)(2,1)S(1)}, u32[]{:S(2)}, u32[]{:S(2)}) collective-permute-start(bf16[1,4,128,512]{3,2,0,1:T(8,128)(2,1)S(1)} %get-tuple-element.11), channel_id=1, source_target_pairs={{0,6},{1,7},{2,4},{3,5},{4,2},{5,3},{6,0},{7,1},{8,14},{9,15},{10,... | collective-permute-start | bytes 1572872 | tf_op jit(solution)/shard_map/ppermute | solution.py:75
  117.5 83.7 %collective-permute-start.6 = (bf16[1,4,128,512]{3,2,0,1:T(8,128)(2,1)S(1)}, bf16[1,4,128,512]{3,2,0,1:T(8,128)(2,1)S(1)}, u32[]{:S(2)}, u32[]{:S(2)}) collective-permute-start(bf16[1,4,128,512]{3,2,0,1:T(8,128)(2,1)S(1)} %get-tuple-element.10), channel_id=1, source_target_pairs={{0,7},{1,6},{2,5},{3,4},{4,3},{5,2},{6,1},{7,0},{8,15},{9,14},{10,... | collective-permute-start | bytes 1572872 | tf_op jit(solution)/shard_map/ppermute | solution.py:75
  201.2 2.0 copy-start
  282.8 16.6 %copy-start.8 = (bf16[1024,512]{1,0:T(8,128)(2,1)S(1)}, bf16[1024,512]{1,0:T(8,128)(2,1)}, u32[]{:S(2)}) copy-start(bf16[1024,512]{1,0:T(8,128)(2,1)} %all-reduce.3.cloned.1.call-done) | copy-start | bytes 3145732
  299.4 11.5 %copy-start.2 = (f32[4,512,512]{2,1,0:T(8,128)S(1)}, f32[4,512,512]{2,1,0:T(8,128)}, u32[]{:S(2)}) copy-start(f32[4,512,512]{2,1,0:T(8,128)} %param.12) | copy-start | bytes 12582916
  310.9 2.4 copy-start.9
  316.1 98.5 %all-to-all-start.1 = ((bf16[8,513,512]{2,1,0:T(8,128)(2,1)}), bf16[8,513,512]{2,1,0:T(8,128)(2,1)}, u32[]{:S(2)}, u32[]{:S(2)}) async-start(bf16[8,513,512]{2,1,0:T(8,128)(2,1)} %pad_maximum_fusion), calls=%async_computation.1 | async-start | bytes 8519680 | tf_op jit(solution)/shard_map/all_to_all | solution.py:103
  320.6 60.0 %all-reduce.5.cloned.1.call-start = ((), (), s32[]{:S(2)}) async-start(), calls=%async_computation.3 | async-start | bytes 4194304 | tf_op jit(solution)/shard_map/psum | solution.py:93
  327.9 54.9 %copy-start.7 = (f32[4,512]{1,0:T(4,128)S(1)}, f32[4,512]{1,0:T(4,128)}, u32[]{:S(2)}) copy-start(f32[4,512]{1,0:T(4,128)} %param.13) | copy-start | bytes 24580
Sparse Core Ops, SparseCore 0:
  50.5 232.2 all-reduce.2
  328.0 52.6 all-reduce.4
